TPU v7x, 512 devices: a whole 4x4x16 slice. The times are simulated.
512 devices in a mesh: seq: 64 (over y, z_hi, x, core), head: 8 (over z_lo).
Axes of the slice: x: 4, y: 4, z: 16 (z_hi: 2, z_lo: 8; z = z_hi * 8 + z_lo), core: 2. Of those that a mesh axis runs over, the one named last changes fastest.
Arguments:
- cross_q: bfloat16 [512, 2048], P('seq', 'head'), may hold values from -20 to 20
- cross_out: bfloat16 [512, 2048], P('seq', 'head'), may hold values from -0.59765625 to 0.59765625
- cross_grad: bfloat16 [512, 2048], P('seq', 'head'), may hold values from -1800 to 1800
- prefix_k: bfloat16 [8192, 2048], P('seq', 'head'), may hold values from -6 to 6
- prefix_v: bfloat16 [8192, 2048], P('seq', 'head'), may hold values from -6 to 6
- pad_counts: int32 [64], P('seq'), may hold values from 0 to 64, as said below
- self_q: bfloat16 [512, 2048], P(('seq', 'head')), may hold values from -20 to 20
- self_k: bfloat16 [512, 2048], P(('seq', 'head')), may hold values from -6 to 6
- self_v: bfloat16 [512, 2048], P(('seq', 'head')), may hold values from -6 to 6
- self_grad: bfloat16 [512, 2048], P(('seq', 'head')), may hold values from -12 to 12
Outputs:
- cross_dq: bfloat16 [512, 2048], P('seq', 'head')
- prefix_dk: bfloat16 [8192, 2048], P('seq', 'head')
- prefix_dv: bfloat16 [8192, 2048], P('seq', 'head')
- self_dq: bfloat16 [512, 2048], P('seq', 'head')
- self_dk: bfloat16 [512, 2048], P('seq', 'head')
- self_dv: bfloat16 [512, 2048], P('seq', 'head')
Inputs may be any that keep to these rules, and one draw needn't show every extreme that they name: `pad_counts`: every shard keeps at least 64 valid tokens; some shard has exactly 64 padded tokens.
All inputs are finite; a program needn't handle non-finite values.
Results may differ from a plain program's by a relative error of at most 0.0086.
Values may be sent and summed in bfloat16 or wider, within the bound.
No kernel may reach another device: no remote copies, remote signals or barrier semaphores. Data moves between devices by JAX's collectives and lax.ppermute only.
A program may use at most 64 MiB of HBM per device.

v0:
```python
import jax
import jax.numpy as jnp
from jax import lax
from jax.sharding import PartitionSpec as P

HEAD_DIM = 128


def in_one_piece(arrays, axis, dim, along):
    ends, at = ([], 0)
    for a in arrays[:-1]:
        at += a.shape[along]
        ends.append(at)
    both = jnp.concatenate(arrays, axis=along)
    return tuple(jnp.split(lax.all_gather(both, axis, axis=dim, tiled=True), ends, axis=along))


def from_everyone(x, axis):
    copies = jnp.broadcast_to(x, (lax.axis_size(axis), *x.shape))
    return lax.all_to_all(copies, axis, split_axis=0, concat_axis=0, tiled=True)


def all_in_one(x, axis):
    leaves = jax.tree.leaves(x)
    order = sorted(range(len(leaves)), key=lambda k: -leaves[k].size)
    width = (1, *leaves[order[0]].shape)[-1]
    lines = [
        jnp.pad(leaves[k].reshape(-1), (0, -leaves[k].size % width)).reshape(-1, width)
        for k in order
    ]
    both, at, found = (from_everyone(jnp.concatenate(lines), axis), 0, {})
    for k, line in zip(order, lines):
        section = both[:, at : at + len(line)].reshape(len(both), -1)
        found[k] = section[:, : leaves[k].size].reshape(-1, *leaves[k].shape)
        at += len(line)
    numbers = iter(range(len(leaves)))
    return jax.tree.map(lambda _: found[next(numbers)], x)


def joined_by_halves(pieces, combine):
    while len(jax.tree.leaves(pieces)[0]) > 1:
        pieces = jax.vmap(combine)(
            *(jax.tree.map(lambda part: part[side::2], pieces) for side in (0, 1))
        )
    return jax.tree.map(lambda part: part[0], pieces)


def merged(x, axis, combine):
    pieces = all_in_one(x, axis)
    return joined_by_halves(pieces, combine)


def split_up(x, dim, size):
    before, after = (x.shape[:dim], x.shape[dim + 1 :])
    return jnp.moveaxis(x.reshape(*before, size, -1, *after), dim, 0)


def sum_at_owner(x, axis, dim):
    size = lax.axis_size(axis)
    parts = lax.all_to_all(split_up(x, dim, size), axis, 0, 0, tiled=True)
    return jnp.sum(parts, axis=0)


def joined_along(parts, dim):
    lengths = list(parts.shape[1:])
    lengths[dim] *= parts.shape[0]
    return jnp.moveaxis(parts, 0, dim).reshape(lengths)


def gathered_copies(x, axis, dim):
    return joined_along(from_everyone(x, axis), dim)


def merge_stats(left_stats, right_stats):
    row_max = jnp.maximum(left_stats[0], right_stats[0])
    row_sum = left_stats[1] * jnp.exp(left_stats[0] - row_max) + right_stats[1] * jnp.exp(
        right_stats[0] - row_max
    )
    return (row_max, row_sum)


def head_scores(queries, key_rows, score_scale):
    return (
        jnp.einsum("qhd,khd->hqk", queries, key_rows, preferred_element_type=jnp.float32)
        * score_scale
    )


def scores_grad(weights, grad_rows, value_rows, row_dot, score_scale):
    grad_probs = jnp.einsum(
        "qhd,khd->hqk", grad_rows, value_rows, preferred_element_type=jnp.float32
    )
    return (weights * (grad_probs - jnp.transpose(row_dot)[:, :, None]) * score_scale).astype(
        jnp.bfloat16
    )


def contract_rows(left_rows, right_rows):
    return jnp.einsum("hqk,qhd->khd", left_rows, right_rows, preferred_element_type=jnp.float32)


def contract_cols(left_rows, right_rows):
    return jnp.einsum("hqk,khd->qhd", left_rows, right_rows, preferred_element_type=jnp.float32)


SEQ_PARTS = ("c", "x", "zh", "y")


def gather_seq(x, dim):
    for axis in SEQ_PARTS:
        x = lax.all_gather(x, axis, axis=dim, tiled=True)
    return x


def merged_seq(row_max, row_sum):
    for axis in SEQ_PARTS:
        both = lax.all_gather(jnp.stack([row_max, row_sum]), axis)
        top = jnp.max(both[:, 0], axis=0)
        row_sum = jnp.sum(both[:, 1] * jnp.exp(both[:, 0] - top), axis=0)
        row_max = top
    return (row_max, row_sum)


def shards(
    cross_q,
    cross_out,
    cross_grad,
    prefix_k,
    prefix_v,
    pad_counts,
    self_q,
    self_k,
    self_v,
    self_grad,
):
    score_scale = HEAD_DIM ** (-0.5)
    own_rows, feature_width = cross_q.shape
    local_heads = feature_width // HEAD_DIM
    tokens = prefix_k.shape[0]
    grad_own = cross_grad.reshape(own_rows, local_heads, HEAD_DIM).astype(jnp.float32)
    out_own = cross_out.reshape(own_rows, local_heads, HEAD_DIM).astype(jnp.float32)
    row_dot = jnp.sum(grad_own * out_own, axis=2).astype(jnp.bfloat16)
    stacked = jnp.stack([self_q, self_k, self_v, self_grad])
    regrouped = lax.all_to_all(stacked, "zl", split_axis=2, concat_axis=1, tiled=True)
    block_rows = regrouped.shape[1]
    self_cols = jnp.transpose(regrouped, (1, 0, 2)).reshape(block_rows, -1)
    pieces = (cross_q, cross_grad, row_dot, self_cols)
    ends, at = ([], 0)
    for piece in pieces[:-1]:
        at += piece.shape[1]
        ends.append(at)
    gathered = gather_seq(jnp.concatenate(pieces, axis=1), 0)
    query_all, grad_all, dots_all, self_all = jnp.split(gathered, ends, axis=1)
    latents = query_all.shape[0]
    query_heads = query_all.reshape(latents, local_heads, HEAD_DIM)
    grad_heads = grad_all.reshape(latents, local_heads, HEAD_DIM)
    key_heads = prefix_k.reshape(tokens, local_heads, HEAD_DIM)
    value_heads = prefix_v.reshape(tokens, local_heads, HEAD_DIM)
    valid_keys = jnp.arange(tokens) < tokens - pad_counts[0]
    scores = head_scores(query_heads, key_heads, score_scale)
    scores = jnp.where(valid_keys[None, None, :], scores, -jnp.inf)
    row_max = jnp.max(scores, axis=2)
    row_sum = jnp.sum(jnp.exp(scores - row_max[:, :, None]), axis=2)
    row_maxes, row_sums = merged_seq(row_max, row_sum)
    log_total = row_maxes + jnp.log(row_sums)
    row_dots = dots_all.astype(jnp.float32)
    weights = jnp.exp(scores - log_total[:, :, None])
    prefix_dv = (
        contract_rows(weights.astype(jnp.bfloat16), grad_heads)
        .reshape(tokens, feature_width)
        .astype(jnp.bfloat16)
    )
    grad_scores = scores_grad(weights, grad_heads, value_heads, row_dots, score_scale)
    prefix_dk = (
        contract_rows(grad_scores, query_heads).reshape(tokens, feature_width).astype(jnp.bfloat16)
    )
    partial_value = contract_cols(grad_scores, key_heads).reshape(latents, feature_width)
    cross_dq = sum_at_owner(partial_value, SEQ_AXES, 0).astype(jnp.bfloat16)
    everything = jnp.transpose(self_all.reshape(latents, 4, feature_width), (1, 0, 2))
    row_start = lax.axis_index(SEQ_AXES) * block_rows
    all_rows = everything.shape[1]
    query_every = everything[0].reshape(all_rows, local_heads, HEAD_DIM)
    key_every = everything[1].reshape(all_rows, local_heads, HEAD_DIM)
    value_every = everything[2].reshape(all_rows, local_heads, HEAD_DIM)
    grad_every = everything[3].reshape(all_rows, local_heads, HEAD_DIM)
    row_ids = jnp.arange(all_rows)
    causal_full = row_ids[:, None] >= row_ids[None, :]
    full_scores = head_scores(query_every, key_every, score_scale)
    full_scores = jnp.where(causal_full[None, :, :], full_scores, -jnp.inf)
    full_lse = jax.nn.logsumexp(full_scores, axis=2)
    full_weights = jnp.exp(full_scores - full_lse[:, :, None])
    full_half = full_weights.astype(jnp.bfloat16)
    full_out = contract_cols(full_half, value_every)
    full_dot = jnp.sum(grad_every.astype(jnp.float32) * full_out, axis=2)
    full_gs = scores_grad(full_weights, grad_every, value_every, full_dot, score_scale)
    query_part = lax.dynamic_slice_in_dim(full_gs, row_start, block_rows, 1)
    self_dq = (
        contract_cols(query_part, key_every).reshape(block_rows, feature_width).astype(jnp.bfloat16)
    )
    key_part = lax.dynamic_slice_in_dim(full_gs, row_start, block_rows, 2)
    half_part = lax.dynamic_slice_in_dim(full_half, row_start, block_rows, 2)
    self_dk = (
        contract_rows(key_part, query_every).reshape(block_rows, feature_width).astype(jnp.bfloat16)
    )
    self_dv = (
        contract_rows(half_part, grad_every).reshape(block_rows, feature_width).astype(jnp.bfloat16)
    )
    return (cross_dq, prefix_dk, prefix_dv, self_dq, self_dk, self_dv)


SEQ_AXES = ("y", "zh", "x", "c")


def solution(mesh):
    sizes = dict(mesh.shape)
    split = mesh.devices.reshape(4, 2, 4, 2, sizes["head"])
    mesh = jax.sharding.Mesh(split, (*SEQ_AXES, "zl"))
    in_specs = (
        P(SEQ_AXES, "zl"),
        P(SEQ_AXES, "zl"),
        P(SEQ_AXES, "zl"),
        P(SEQ_AXES, "zl"),
        P(SEQ_AXES, "zl"),
        P(SEQ_AXES),
        P((*SEQ_AXES, "zl"), None),
        P((*SEQ_AXES, "zl"), None),
        P((*SEQ_AXES, "zl"), None),
        P((*SEQ_AXES, "zl"), None),
    )
    out_specs = (
        P(SEQ_AXES, "zl"),
        P(SEQ_AXES, "zl"),
        P(SEQ_AXES, "zl"),
        P(SEQ_AXES, "zl"),
        P(SEQ_AXES, "zl"),
        P(SEQ_AXES, "zl"),
    )
    return jax.shard_map(shards, mesh=mesh, in_specs=in_specs, out_specs=out_specs, check_vma=False)
```

profile of v0, /device:TPU:33, one launch (start us, length us, event | category | flops | bytes accessed | tf_op | source)
XLA Modules:
  0.0 228.5 jit_solution(2826771414848816739)
XLA Ops:
  7.2 0.0 copy-start
  7.2 0.0 copy-start.3
  7.2 0.0 copy-start.4
  7.2 0.8 pad_maximum_fusion
  8.0 0.9 copy.128
  9.0 0.5 broadcast.35
  9.5 0.0 copy-start.5
  9.5 11.6 %reduce.4 = bf16[2048,4]{1,0:T(8,128)(2,1)S(1)} reduce(bf16[2048,1,4]{2,1,0:T(2,128)(2,1)S(1)} %bitcast.168, bf16[]{:T(256)} %broadcast.35), dimensions={1}, to_apply=%bitcast.135.reduce_sub_computation | reduce | bytes 32770
  21.1 1.4 reshape.100
  22.5 12.1 %all-to-all-start = ((bf16[8,2,512]{2,1,0:T(2,128)(2,1)}), bf16[8,2,512]{2,1,0:T(2,128)(2,1)S(1)}, u32[]{:S(2)}, u32[]{:S(2)}) async-start(bf16[8,2,512]{2,1,0:T(2,128)(2,1)} %reshape.100), calls=%async_computation | async-start | bytes 32768 | tf_op jit(solution)/shard_map/all_to_all | solution.py:144
  34.5 0.0 all-gather.6.cloned.1.call-start
  34.5 0.0 copy-done.3
  34.5 0.0 copy-done.4
  34.6 0.1 bitcast_reduce_fusion.4
  34.6 0.1 copy.130
  34.7 7.9 %all-to-all-done = bf16[8,2,512]{2,1,0:T(2,128)(2,1)S(1)} async-done(((bf16[8,2,512]{2,1,0:T(2,128)(2,1)}), bf16[8,2,512]{2,1,0:T(2,128)(2,1)S(1)}, u32[]{:S(2)}, u32[]{:S(2)}) %all-to-all-start) | async-done | bytes 16416 | tf_op jit(solution)/shard_map/all_to_all | solution.py:144
  42.7 1.4 reshape.101
  44.1 0.6 copy.129
  44.6 0.0 copy-done.5
  44.7 0.1 concatenate.3
  44.8 3.6 %all_gather.36 = bf16[16,1538]{1,0:T(8,128)(2,1)S(1)} all-gather(bf16[8,1538]{1,0:T(8,128)(2,1)S(1)} %concatenate.3), channel_id=1, replica_groups=mesh['y'=4,'zh'=2,'x'=4,'c'=2,'zl'=8] {'c'}, dimensions={0}, use_global_device_ids=true | all-gather | bytes 73824 | tf_op jit(solution)/shard_map/all_gather | solution.py:111
  48.4 10.1 %all_gather.37 = bf16[64,1538]{1,0:T(8,128)(2,1)S(1)} all-gather(bf16[16,1538]{1,0:T(8,128)(2,1)S(1)} %all_gather.36), channel_id=1, replica_groups=mesh['y'=4,'zh'=2,'x'=4,'c'=2,'zl'=8] {'x'}, dimensions={0}, use_global_device_ids=true | all-gather | bytes 246080 | tf_op jit(solution)/shard_map/all_gather | solution.py:111
  58.4 30.3 %all_gather.38 = bf16[128,1538]{1,0:T(8,128)(2,1)} all-gather(bf16[64,1538]{1,0:T(8,128)(2,1)S(1)} %all_gather.37), channel_id=1, replica_groups=mesh['y'=4,'zh'=2,'x'=4,'c'=2,'zl'=8] {'zh'}, dimensions={0}, use_global_device_ids=true | all-gather | bytes 590592 | tf_op jit(solution)/shard_map/all_gather | solution.py:111
  88.8 0.0 all-gather.6.cloned.1.call-update
  89.5 0.1 iota_compare_fusion
  89.5 30.5 %all-gather.6.cloned.1.call-done = bf16[512,1538]{1,0:T(8,128)(2,1)} async-done(((bf16[128,1538]{1,0:T(8,128)(2,1)}), bf16[512,1538]{1,0:T(8,128)(2,1)}) %all-gather.6.cloned.1.call-update) | async-done | bytes 1574928 | tf_op jit(solution)/shard_map/all_gather | solution.py:111
  120.0 0.9 convert_bitcast_fusion
  121.0 0.1 copy.141
  121.1 1.1 fusion.37
  122.2 0.0 copy-start.2
  122.2 0.1 copy.131
  122.3 0.1 copy.138
  122.5 0.0 copy-done
  122.5 0.2 fusion.39
  122.7 0.0 copy-start.1
  122.7 0.1 exponential_reduce_fusion.1
  122.8 2.3 %all-gather = f32[4,2,512]{2,1,0:T(2,128)S(1)} all-gather(f32[2,2,512]{2,1,0:T(2,128)S(1)} %pad_maximum_fusion.1), channel_id=2, replica_groups=mesh['y'=4,'zh'=2,'x'=4,'c'=2,'zl'=8] {'c'}, dimensions={0}, use_global_device_ids=true | all-gather | bytes 24576 | tf_op jit(solution)/shard_map/all_gather | solution.py:117
  125.2 9.3 %all-gather.1 = f32[8,2,512]{2,1,0:T(2,128)S(1)} all-gather(f32[2,2,512]{2,1,0:T(2,128)S(1)} %pad_maximum_fusion.2), channel_id=3, replica_groups=mesh['y'=4,'zh'=2,'x'=4,'c'=2,'zl'=8] {'x'}, dimensions={0}, use_global_device_ids=true | all-gather | bytes 40960 | tf_op jit(solution)/shard_map/all_gather | solution.py:117
  134.6 11.9 %all-gather.2 = f32[4,2,512]{2,1,0:T(2,128)S(1)} all-gather(f32[2,2,512]{2,1,0:T(2,128)S(1)} %pad_maximum_fusion.3), channel_id=4, replica_groups=mesh['y'=4,'zh'=2,'x'=4,'c'=2,'zl'=8] {'zh'}, dimensions={0}, use_global_device_ids=true | all-gather | bytes 24576 | tf_op jit(solution)/shard_map/all_gather | solution.py:117
  146.6 9.0 %all-gather.3 = f32[8,2,512]{2,1,0:T(2,128)S(1)} all-gather(f32[2,2,512]{2,1,0:T(2,128)S(1)} %pad_maximum_fusion.4), channel_id=5, replica_groups=mesh['y'=4,'zh'=2,'x'=4,'c'=2,'zl'=8] {'y'}, dimensions={0}, use_global_device_ids=true | all-gather | bytes 40960 | tf_op jit(solution)/shard_map/all_gather | solution.py:117
  155.7 0.3 convolution_convert_fusion
  155.9 0.0 copy-done.2
  155.9 0.2 fusion.5
  156.1 0.2 convolution_convert_fusion.1
  156.4 0.3 convolution_bitcast_fusion.1
  156.7 0.0 copy-done.1
  156.7 0.6 split.19
  157.3 0.5 copy.177
  157.9 0.1 fusion.38
  157.9 0.7 copy.159
  158.7 0.7 copy.160
  159.4 0.4 copy.145
  159.8 1.2 reshape_reshape.3
  161.0 21.8 %all-to-all-start.1 = ((f32[64,8,256]{2,1,0:T(8,128)}), f32[64,8,256]{2,1,0:T(8,128)S(1)}, u32[]{:S(2)}, u32[]{:S(2)}) async-start(f32[64,8,256]{2,1,0:T(8,128)} %reshape_reshape.3), calls=%async_computation.1 | async-start | bytes 1048576 | tf_op jit(solution)/shard_map/all_to_all | solution.py:60
  182.9 0.6 fusion.40
  183.5 0.3 exponential_reduce_fusion
  183.8 0.3 fusion
  184.1 0.8 fusion.8
  184.9 0.3 fusion.6
  185.2 0.6 multiply_convert_fusion
  185.9 0.8 fusion.7
  186.6 1.0 fusion.9
  187.6 33.4 %all-to-all-done.1 = f32[64,8,256]{2,1,0:T(8,128)S(1)} async-done(((f32[64,8,256]{2,1,0:T(8,128)}), f32[64,8,256]{2,1,0:T(8,128)S(1)}, u32[]{:S(2)}, u32[]{:S(2)}) %all-to-all-start.1) | async-done | bytes 524320 | tf_op jit(solution)/shard_map/all_to_all | solution.py:60
  221.0 0.7 reduce_sum.87
  (17 shorter events, 0.2 us)
Async XLA Ops:
  7.2 115.3 %copy-start = (bf16[128,256]{1,0:T(8,128)(2,1)S(1)}, bf16[128,256]{1,0:T(8,128)(2,1)}, u32[]{:S(2)}) copy-start(bf16[128,256]{1,0:T(8,128)(2,1)} %param.13) | copy-start | bytes 196612
  7.2 27.4 %copy-start.3 = (bf16[8,256]{1,0:T(8,128)(2,1)S(1)}, bf16[8,256]{1,0:T(8,128)(2,1)}, u32[]{:S(2)}) copy-start(bf16[8,256]{1,0:T(8,128)(2,1)} %param.12) | copy-start | bytes 12292
  7.2 27.4 %copy-start.4 = (bf16[8,256]{1,0:T(8,128)(2,1)S(1)}, bf16[8,256]{1,0:T(8,128)(2,1)}, u32[]{:S(2)}) copy-start(bf16[8,256]{1,0:T(8,128)(2,1)} %param.11) | copy-start | bytes 12292
  9.5 35.2 %copy-start.5 = (bf16[8,256]{1,0:T(8,128)(2,1)S(1)}, bf16[8,256]{1,0:T(8,128)(2,1)}, u32[]{:S(2)}) copy-start(bf16[8,256]{1,0:T(8,128)(2,1)} %param.10) | copy-start | bytes 12292
  22.5 20.2 %all-to-all-start = ((bf16[8,2,512]{2,1,0:T(2,128)(2,1)}), bf16[8,2,512]{2,1,0:T(2,128)(2,1)S(1)}, u32[]{:S(2)}, u32[]{:S(2)}) async-start(bf16[8,2,512]{2,1,0:T(2,128)(2,1)} %reshape.100), calls=%async_computation | async-start | bytes 32768 | tf_op jit(solution)/shard_map/all_to_all | solution.py:144
  34.5 85.5 %all-gather.6.cloned.1.call-start = ((), (), s32[]{:S(2)}) async-start(), calls=%async_computation.2 | async-start | bytes 2129920 | tf_op jit(solution)/shard_map/all_gather | solution.py:111
  122.2 33.8 %copy-start.2 = (bf16[128,256]{1,0:T(8,128)(2,1)S(1)}, bf16[128,256]{1,0:T(8,128)(2,1)}, u32[]{:S(2)}) copy-start(bf16[128,256]{1,0:T(8,128)(2,1)} %param.14) | copy-start | bytes 196612
  122.7 34.0 %copy-start.1 = (bf16[512,1538]{1,0:T(8,128)(2,1)S(1)}, bf16[512,1538]{1,0:T(8,128)(2,1)}, u32[]{:S(2)}) copy-start(bf16[512,1538]{1,0:T(8,128)(2,1)} %all-gather.6.cloned.1.call-done) | copy-start | bytes 4724740
  161.0 59.9 %all-to-all-start.1 = ((f32[64,8,256]{2,1,0:T(8,128)}), f32[64,8,256]{2,1,0:T(8,128)S(1)}, u32[]{:S(2)}, u32[]{:S(2)}) async-start(f32[64,8,256]{2,1,0:T(8,128)} %reshape_reshape.3), calls=%async_computation.1 | async-start | bytes 1048576 | tf_op jit(solution)/shard_map/all_to_all | solution.py:60
Sparse Core Ops, SparseCore 0:
  88.9 31.0 all-gather.5
where the time goes:
time: 229 us; the launch traced here: 228 us
  blocking collectives  76.6 us (33%)
  waiting for transfers between devices  71.8 us (31%)
  starting transfers between devices  33.9 us (15%)
  other arithmetic  15.1 us (7%)
  between operations  15 us (7%)
  local copies, waits for them, and re-layouts  10.9 us (5%)
  matrix products  5.29 us (2%)
    all_gather x3, blocking collectives, gather_seq(): x = lax.all_gather(x, axis, axis=dim, tiled=True)  44 us
    all_to_all x1, waiting for transfers between devices, sum_at_owner(): parts = lax.all_to_all(split_up(x, dim, size), axis, 0, 0, tiled=True)  33.4 us
    all_gather x4, blocking collectives, merged_seq(): both = lax.all_gather(jnp.stack([row_max, row_sum]), axis)  32.6 us
    all_gather x1, waiting for transfers between devices, gather_seq(): x = lax.all_gather(x, axis, axis=dim, tiled=True)  30.5 us
    all_to_all x1, starting transfers between devices, sum_at_owner(): parts = lax.all_to_all(split_up(x, dim, size), axis, 0, 0, tiled=True)  21.8 us
    all_to_all x1, starting transfers between devices, shards(): lax.all_to_all(stacked, 'zl', split_axis=2, concat_axis=1, tiled=True)  12.1 us
    unnamed x1, other arithmetic  11.6 us
    all_to_all x1, waiting for transfers between devices, shards(): lax.all_to_all(stacked, 'zl', split_axis=2, concat_axis=1, tiled=True)  7.93 us
  transfers between devices with their start and end apart: 3, of which 3 were waited for; matrix products, arithmetic and copies ran while one was open for 2% of the time, Pallas kernels for 0%

commit v1 on v0

--- a/solution.py
+++ b/solution.py
@@ -141,7 +141,10 @@
     out_own = cross_out.reshape(own_rows, local_heads, HEAD_DIM).astype(jnp.float32)
     row_dot = jnp.sum(grad_own * out_own, axis=2).astype(jnp.bfloat16)
     stacked = jnp.stack([self_q, self_k, self_v, self_grad])
-    regrouped = lax.all_to_all(stacked, "zl", split_axis=2, concat_axis=1, tiled=True)
+    regrouped = jnp.concatenate(
+        lax.all_to_all(jnp.stack(jnp.split(stacked, lax.axis_size("zl"), axis=2)), "zl", 0, 0),
+        axis=1,
+    )
     block_rows = regrouped.shape[1]
     self_cols = jnp.transpose(regrouped, (1, 0, 2)).reshape(block_rows, -1)
     pieces = (cross_q, cross_grad, row_dot, self_cols)

time: 229 us -> 220 us (0.961)
  other arithmetic: 15.1 us -> 3.3 us
    unnamed x1 -> x0, other arithmetic: 11.6 us -> none
    unnamed x18 -> x16, local copies, waits for them, and re-layouts: 4.82 us -> 5.57 us
  transfers between devices with their start and end apart: 3 -> 3, of which waited for: 3 -> 3; matrix products, arithmetic and copies ran while one was open for 2% -> 3% of each run, Pallas kernels for 0% -> 0%
where the time goes in v1:
time: 220 us; the launch traced here: 219 us
  blocking collectives  77.7 us (35%)
  waiting for transfers between devices  72.8 us (33%)
  starting transfers between devices  34 us (15%)
  between operations  14.9 us (7%)
  local copies, waits for them, and re-layouts  11.1 us (5%)
  matrix products  5.28 us (2%)
  other arithmetic  3.3 us (2%)
    all_gather x3, blocking collectives, gather_seq(): x = lax.all_gather(x, axis, axis=dim, tiled=True)  43.9 us
    all_gather x4, blocking collectives, merged_seq(): both = lax.all_gather(jnp.stack([row_max, row_sum]), axis)  33.8 us
    all_to_all x1, waiting for transfers between devices, sum_at_owner(): parts = lax.all_to_all(split_up(x, dim, size), axis, 0, 0, tiled=True)  33.4 us
    all_gather x1, waiting for transfers between devices, gather_seq(): x = lax.all_gather(x, axis, axis=dim, tiled=True)  32.2 us
    all_to_all x1, starting transfers between devices, sum_at_owner(): parts = lax.all_to_all(split_up(x, dim, size), axis, 0, 0, tiled=True)  21.9 us
    all_to_all x1, starting transfers between devices, shards(): lax.all_to_all(jnp.stack(jnp.split(stacked, lax.axis_size('zl'), axis=2))...  12.1 us
    all_to_all x1, waiting for transfers between devices, shards(): lax.all_to_all(jnp.stack(jnp.split(stacked, lax.axis_size('zl'), axis=2))...  7.24 us
    unnamed x16, local copies, waits for them, and re-layouts  5.57 us
  transfers between devices with their start and end apart: 3, of which 3 were waited for; matrix products, arithmetic and copies ran while one was open for 3% of the time, Pallas kernels for 0%

profile of v1, /device:TPU:33, one launch (start us, length us, event | category | flops | bytes accessed | tf_op | source)
XLA Modules:
  0.0 219.1 jit_solution(18412205469411828668)
XLA Ops:
  7.2 0.0 copy-start
  7.2 0.8 pad_maximum_fusion
  8.0 0.6 constant_dynamic-update-slice_fusion.7
  8.6 0.6 constant_dynamic-update-slice_fusion.6
  9.2 0.6 constant_dynamic-update-slice_fusion.5
  9.8 0.6 constant_dynamic-update-slice_fusion.4
  10.3 0.6 constant_dynamic-update-slice_fusion.3
  10.9 0.6 constant_dynamic-update-slice_fusion.2
  11.5 0.6 constant_dynamic-update-slice_fusion.1
  12.1 0.6 constant_dynamic-update-slice_fusion
  12.7 12.1 %all-to-all-start = ((bf16[8,4,1,256]{3,1,2,0:T(4,128)(2,1)}), bf16[8,4,1,256]{3,1,2,0:T(4,128)(2,1)S(1)}, u32[]{:S(2)}, u32[]{:S(2)}) async-start(bf16[8,4,1,256]{3,1,2,0:T(4,128)(2,1)} %constant_dynamic-update-slice_fusion), calls=%async_computation | async-start | bytes 32768 | tf_op jit(solution)/shard_map/all_to_all | solution.py:145
  24.7 0.0 all-gather.6.cloned.1.call-start
  24.7 0.8 bitcast_reduce_fusion.4
  25.5 0.1 copy.101
  25.6 7.2 %all-to-all-done = bf16[8,4,1,256]{3,1,2,0:T(4,128)(2,1)S(1)} async-done(((bf16[8,4,1,256]{3,1,2,0:T(4,128)(2,1)}), bf16[8,4,1,256]{3,1,2,0:T(4,128)(2,1)S(1)}, u32[]{:S(2)}, u32[]{:S(2)}) %all-to-all-start) | async-done | bytes 16416 | tf_op jit(solution)/shard_map/all_to_all | solution.py:145
  32.9 0.8 concatenate.3
  33.7 3.6 %all_gather.36 = bf16[16,1538]{1,0:T(8,128)(2,1)S(1)} all-gather(bf16[8,1538]{1,0:T(8,128)(2,1)S(1)} %concatenate.3), channel_id=1, replica_groups=mesh['y'=4,'zh'=2,'x'=4,'c'=2,'zl'=8] {'c'}, dimensions={0}, use_global_device_ids=true | all-gather | bytes 73824 | tf_op jit(solution)/shard_map/all_gather | solution.py:111
  37.3 10.1 %all_gather.37 = bf16[64,1538]{1,0:T(8,128)(2,1)S(1)} all-gather(bf16[16,1538]{1,0:T(8,128)(2,1)S(1)} %all_gather.36), channel_id=1, replica_groups=mesh['y'=4,'zh'=2,'x'=4,'c'=2,'zl'=8] {'x'}, dimensions={0}, use_global_device_ids=true | all-gather | bytes 246080 | tf_op jit(solution)/shard_map/all_gather | solution.py:111
  47.3 30.2 %all_gather.38 = bf16[128,1538]{1,0:T(8,128)(2,1)S(1)} all-gather(bf16[64,1538]{1,0:T(8,128)(2,1)S(1)} %all_gather.37), channel_id=1, replica_groups=mesh['y'=4,'zh'=2,'x'=4,'c'=2,'zl'=8] {'zh'}, dimensions={0}, use_global_device_ids=true | all-gather | bytes 590592 | tf_op jit(solution)/shard_map/all_gather | solution.py:111
  77.6 0.9 copy.102
  78.5 0.0 all-gather.6.cloned.1.call-update
  78.5 0.0 copy-start.2
  79.2 0.1 iota_compare_fusion
  79.3 32.2 %all-gather.6.cloned.1.call-done = bf16[512,1538]{0,1:T(8,128)(2,1)} async-done(((bf16[128,1538]{0,1:T(8,128)(2,1)}), bf16[512,1538]{0,1:T(8,128)(2,1)}) %all-gather.6.cloned.1.call-update) | async-done | bytes 1574928 | tf_op jit(solution)/shard_map/all_gather | solution.py:111
  111.5 0.0 copy-start.1
  111.5 1.2 fusion.37
  112.7 0.0 copy-done
  112.7 0.2 fusion.39
  113.0 0.1 exponential_reduce_fusion.1
  113.1 3.0 %all-gather = f32[4,2,512]{2,1,0:T(2,128)S(1)} all-gather(f32[2,2,512]{2,1,0:T(2,128)S(1)} %pad_maximum_fusion.1), channel_id=2, replica_groups=mesh['y'=4,'zh'=2,'x'=4,'c'=2,'zl'=8] {'c'}, dimensions={0}, use_global_device_ids=true | all-gather | bytes 24576 | tf_op jit(solution)/shard_map/all_gather | solution.py:117
  116.2 9.6 %all-gather.1 = f32[8,2,512]{2,1,0:T(2,128)S(1)} all-gather(f32[2,2,512]{2,1,0:T(2,128)S(1)} %pad_maximum_fusion.2), channel_id=3, replica_groups=mesh['y'=4,'zh'=2,'x'=4,'c'=2,'zl'=8] {'x'}, dimensions={0}, use_global_device_ids=true | all-gather | bytes 40960 | tf_op jit(solution)/shard_map/all_gather | solution.py:117
  125.8 11.9 %all-gather.2 = f32[4,2,512]{2,1,0:T(2,128)S(1)} all-gather(f32[2,2,512]{2,1,0:T(2,128)S(1)} %pad_maximum_fusion.3), channel_id=4, replica_groups=mesh['y'=4,'zh'=2,'x'=4,'c'=2,'zl'=8] {'zh'}, dimensions={0}, use_global_device_ids=true | all-gather | bytes 24576 | tf_op jit(solution)/shard_map/all_gather | solution.py:117
  137.8 9.2 %all-gather.3 = f32[8,2,512]{2,1,0:T(2,128)S(1)} all-gather(f32[2,2,512]{2,1,0:T(2,128)S(1)} %pad_maximum_fusion.4), channel_id=5, replica_groups=mesh['y'=4,'zh'=2,'x'=4,'c'=2,'zl'=8] {'y'}, dimensions={0}, use_global_device_ids=true | all-gather | bytes 40960 | tf_op jit(solution)/shard_map/all_gather | solution.py:117
  147.1 0.2 convolution_convert_fusion
  147.3 0.0 copy-done.1
  147.4 0.0 copy-done.2
  147.4 0.2 fusion.5
  147.6 0.2 convolution_convert_fusion.1
  147.8 0.3 convolution_bitcast_fusion.1
  148.1 0.2 split.59
  148.4 0.1 fusion.38
  148.4 0.7 copy.127
  149.2 0.7 copy.128
  149.9 0.4 copy.114
  150.3 1.2 reshape_reshape.3
  151.5 21.9 %all-to-all-start.1 = ((f32[64,8,256]{2,1,0:T(8,128)}), f32[64,8,256]{2,1,0:T(8,128)S(1)}, u32[]{:S(2)}, u32[]{:S(2)}) async-start(f32[64,8,256]{2,1,0:T(8,128)} %reshape_reshape.3), calls=%async_computation.1 | async-start | bytes 1048576 | tf_op jit(solution)/shard_map/all_to_all | solution.py:60
  173.5 0.6 fusion.40
  174.1 0.3 exponential_reduce_fusion
  174.4 0.3 fusion
  174.8 0.8 fusion.8
  175.5 0.3 fusion.6
  175.9 0.6 multiply_convert_fusion
  176.5 0.8 fusion.7
  177.3 1.0 fusion.9
  178.2 33.4 %all-to-all-done.1 = f32[64,8,256]{2,1,0:T(8,128)S(1)} async-done(((f32[64,8,256]{2,1,0:T(8,128)}), f32[64,8,256]{2,1,0:T(8,128)S(1)}, u32[]{:S(2)}, u32[]{:S(2)}) %all-to-all-start.1) | async-done | bytes 524320 | tf_op jit(solution)/shard_map/all_to_all | solution.py:60
  211.6 0.7 reduce_sum.87
  (18 shorter events, 0.2 us)
Async XLA Ops:
  7.2 105.6 %copy-start = (bf16[128,256]{1,0:T(8,128)(2,1)S(1)}, bf16[128,256]{1,0:T(8,128)(2,1)}, u32[]{:S(2)}) copy-start(bf16[128,256]{1,0:T(8,128)(2,1)} %param.13) | copy-start | bytes 196612
  12.7 20.2 %all-to-all-start = ((bf16[8,4,1,256]{3,1,2,0:T(4,128)(2,1)}), bf16[8,4,1,256]{3,1,2,0:T(4,128)(2,1)S(1)}, u32[]{:S(2)}, u32[]{:S(2)}) async-start(bf16[8,4,1,256]{3,1,2,0:T(4,128)(2,1)} %constant_dynamic-update-slice_fusion), calls=%async_computation | async-start | bytes 32768 | tf_op jit(solution)/shard_map/all_to_all | solution.py:145
  24.7 86.8 %all-gather.6.cloned.1.call-start = ((), (), s32[]{:S(2)}) async-start(), calls=%async_computation.2 | async-start | bytes 1976320 | tf_op jit(solution)/shard_map/all_gather | solution.py:111
  78.5 68.8 %copy-start.2 = (bf16[128,256]{1,0:T(8,128)(2,1)S(1)}, bf16[128,256]{1,0:T(8,128)(2,1)}, u32[]{:S(2)}) copy-start(bf16[128,256]{1,0:T(8,128)(2,1)} %param.14) | copy-start | bytes 196612
  111.5 35.8 %copy-start.1 = (bf16[512,1538]{0,1:T(8,128)(2,1)S(1)}, bf16[512,1538]{0,1:T(8,128)(2,1)}, u32[]{:S(2)}) copy-start(bf16[512,1538]{0,1:T(8,128)(2,1)} %all-gather.6.cloned.1.call-done) | copy-start | bytes 4724740
  151.5 60.1 %all-to-all-start.1 = ((f32[64,8,256]{2,1,0:T(8,128)}), f32[64,8,256]{2,1,0:T(8,128)S(1)}, u32[]{:S(2)}, u32[]{:S(2)}) async-start(f32[64,8,256]{2,1,0:T(8,128)} %reshape_reshape.3), calls=%async_computation.1 | async-start | bytes 1048576 | tf_op jit(solution)/shard_map/all_to_all | solution.py:60
Sparse Core Ops, SparseCore 0:
  78.6 32.8 all-gather.5
